TPU v7x, 128 devices: a whole 4x4x4 slice. The times are simulated.
128 devices in a mesh: node: 8 (over x, core), dev: 16 (over z, y).
Axes of the slice: x: 4, y: 4, z: 4, core: 2. Of those that a mesh axis runs over, the one named last changes fastest.
Arguments:
- tokens: bfloat16 [32768, 7168], P(('node', 'dev')), may hold values from -6 to 6
- grad_out: bfloat16 [32768, 7168], P(('node', 'dev')), may hold values from -1.796875 to 1.796875
- router_gates: bfloat16 [32768, 8], P(('node', 'dev')), may hold values from 0.049804688 to 1
- expert_ids: int32 [32768, 8], P(('node', 'dev')), may hold values from 0 to 255, as said below
- slot_plan: int32 [256, 2], replicated, may hold values from 0 to 16, as said below
- w_gate: bfloat16 [8, 7168, 2048], P(None, 'dev', 'node'), may hold values from -0.0625 to 0.0625
- w_up: bfloat16 [8, 7168, 2048], P(None, 'dev', 'node'), may hold values from -0.0625 to 0.0625
- w_down: bfloat16 [8, 2048, 7168], P(None, 'node', 'dev'), may hold values from -0.125 to 0.125
Outputs:
- grad_tokens: bfloat16 [32768, 7168], P(('node', 'dev'))
- grad_gates: float32 [32768, 8], P(('node', 'dev'))
- grad_w_gate: bfloat16 [8, 7168, 2048], P(None, 'dev', 'node')
- grad_w_up: bfloat16 [8, 7168, 2048], P(None, 'dev', 'node')
- grad_w_down: bfloat16 [8, 2048, 7168], P(None, 'node', 'dev')
Inputs may be any that keep to these rules, and one draw needn't show every extreme that they name: `expert_ids`: each token names 8 different experts. Within one block of 256 tokens (the tokens of one device), at most 4 pairs name any one expert that has slots, and in every draw one expert that has slots is named exactly 2 * 2 times in every block. `slot_plan`: exactly 8 rows hold slots: each such row holds two different slots, and every slot 0 .. 15 stands in exactly one row. Every entry of the other rows equals 16.
All inputs are finite; a program needn't handle non-finite values.
Results may differ from a plain program's by a relative error of at most 0.0059.
Values may be sent and summed in bfloat16 or wider, within the bound.
No kernel may reach another device: no remote copies, remote signals or barrier semaphores. Data moves between devices by JAX's collectives and lax.ppermute only.
A program may use at most 128 MiB of HBM per device.

v0:
```python
import jax
import jax.numpy as jnp
from jax import lax
from jax.sharding import PartitionSpec as P

TOP = 8
CAP = 2
REPS = 2
LANE = 128


def routing(expert_ids, slot_plan, slot_count, round_total):
    expert_count = slot_plan.shape[0]
    in_round = (slot_plan[:, 0] < slot_count).astype(jnp.int32)
    expert_rank = jnp.cumsum(in_round) - 1
    rank_match = (in_round[:, None] > 0) & (
        expert_rank[:, None] == jnp.arange(round_total, dtype=jnp.int32)[None, :]
    )
    hot_ids = jnp.sum(
        jnp.where(rank_match, jnp.arange(expert_count, dtype=jnp.int32)[:, None], 0), axis=0
    )
    match = expert_ids[:, :, None] == hot_ids[None, None, :]
    named = jnp.sum(match.astype(jnp.int32), axis=1)
    tok_rows = expert_ids.shape[0]
    earlier = (
        jnp.arange(tok_rows, dtype=jnp.int32)[None, :]
        < jnp.arange(tok_rows, dtype=jnp.int32)[:, None]
    ).astype(jnp.bfloat16)
    before = jnp.dot(
        earlier, named.astype(jnp.bfloat16), preferred_element_type=jnp.float32
    ).astype(jnp.int32)
    per_rank = REPS * CAP
    target = per_rank * jnp.arange(round_total, dtype=jnp.int32)[None, :] + before
    return (match, named, target)


def local(tokens, grad_out, router_gates, expert_ids, slot_plan, w_gate, w_up, w_down):
    col_count = lax.axis_size("dev")
    node_count = lax.axis_size("node")
    tok_rows, model_width = tokens.shape
    round_total, chunk, node_hidden = w_gate.shape
    half = node_hidden // REPS
    per_rank = REPS * CAP
    row_slots = round_total * per_rank
    wide = model_width + LANE

    def split_cols(w):
        w = w.reshape(round_total, chunk, REPS, half)
        return jnp.swapaxes(w, 1, 2).reshape(col_count, chunk, half)

    send_wg = split_cols(w_gate)
    send_wu = split_cols(w_up)
    send_wd = split_cols(jnp.swapaxes(w_down, 1, 2))
    slot_gate = lax.all_to_all(send_wg, "dev", 0, 0, tiled=True).reshape(model_width, half)
    slot_up = lax.all_to_all(send_wu, "dev", 0, 0, tiled=True).reshape(model_width, half)
    slot_down_t = lax.all_to_all(send_wd, "dev", 0, 0, tiled=True).reshape(model_width, half)
    match, named, target = routing(expert_ids, slot_plan, col_count, round_total)
    q_ids = jnp.arange(row_slots, dtype=jnp.int32)
    chooser = (named[None, :, :] > 0) & (target[None, :, :] == q_ids[:, None, None])
    pick_rows = jnp.sum(chooser.astype(jnp.float32), axis=-1)
    pick_half = pick_rows.astype(jnp.bfloat16)
    gates_f = router_gates.astype(jnp.float32)
    rank_gate = jnp.sum(jnp.where(match, gates_f[:, :, None], 0.0), axis=1)
    gate_send = jnp.sum(jnp.where(chooser, rank_gate[None, :, :], 0.0), axis=(1, 2)).astype(
        jnp.bfloat16
    )
    x_send = jnp.dot(pick_half, tokens, preferred_element_type=jnp.float32).astype(jnp.bfloat16)
    dy_send = jnp.dot(pick_half, grad_out, preferred_element_type=jnp.float32).astype(jnp.bfloat16)
    gate_block = jnp.where(
        jnp.arange(LANE)[None, :] == 0, gate_send[:, None], jnp.zeros((), jnp.bfloat16)
    )
    dy_send = jnp.concatenate([dy_send, gate_block], axis=1)
    both_send = jnp.concatenate([x_send, dy_send], axis=1)
    both_width = model_width + wide
    both = both_send.reshape(round_total, 1, per_rank, both_width)
    both = jnp.broadcast_to(both, (round_total, REPS, per_rank, both_width))
    both = lax.all_to_all(both.reshape(col_count, per_rank, both_width), "dev", 0, 0, tiled=True)
    both = both.reshape(col_count * per_rank, both_width)
    x_rows = lax.all_gather(both[:, :model_width], "node", axis=0, tiled=True)
    dy_ext = lax.all_gather(both[:, model_width:], "node", axis=0, tiled=True)
    dy_rows = dy_ext[:, :model_width]
    gate_rows = dy_ext[:, model_width].astype(jnp.float32)[:, None]
    gate_pre = jnp.dot(x_rows, slot_gate, preferred_element_type=jnp.float32)
    up_pre = jnp.dot(x_rows, slot_up, preferred_element_type=jnp.float32)
    back_proj = jnp.dot(dy_rows, slot_down_t, preferred_element_type=jnp.float32)
    sigmoid_gate = jax.nn.sigmoid(gate_pre)
    active = gate_pre * sigmoid_gate
    hidden = active * up_pre
    scaled_back = gate_rows * back_proj
    d_gate = (scaled_back * up_pre * sigmoid_gate * (1.0 + gate_pre * (1.0 - sigmoid_gate))).astype(
        jnp.bfloat16
    )
    d_up = (scaled_back * active).astype(jnp.bfloat16)
    scaled_hidden = (gate_rows * hidden).astype(jnp.bfloat16)
    gate_terms = jnp.sum(back_proj * hidden, axis=-1)
    row_count = x_rows.shape[0]
    first_slot = (jnp.arange(row_count, dtype=jnp.int32) % REPS == 0)[:, None]

    def by_slot(d):
        zero = jnp.zeros((), d.dtype)
        return jnp.concatenate(
            [jnp.where(first_slot, d, zero), jnp.where(first_slot, zero, d)], axis=1
        )

    def slot_pair_sum(rows, d):
        acc = jnp.einsum("rd,rh->dh", rows, by_slot(d), preferred_element_type=jnp.float32)
        acc = lax.reduce_precision(acc, exponent_bits=8, mantissa_bits=7)
        return (acc[:, :half] + acc[:, half:]).astype(jnp.bfloat16)

    grad_gate_cols = slot_pair_sum(x_rows, d_gate)
    grad_up_cols = slot_pair_sum(x_rows, d_up)
    grad_down_cols = slot_pair_sum(dy_rows, scaled_hidden)
    pad_rows = ((0, LANE), (0, 0))
    row_ext = jnp.einsum(
        "rh,dh->rd", d_gate, jnp.pad(slot_gate, pad_rows), preferred_element_type=jnp.float32
    )
    row_ext = row_ext + jnp.einsum(
        "rh,dh->rd", d_up, jnp.pad(slot_up, pad_rows), preferred_element_type=jnp.float32
    )
    term_col = jnp.arange(wide, dtype=jnp.int32)[None, :] == model_width
    row_ext = row_ext + jnp.where(term_col, gate_terms[:, None], 0.0)
    summed = lax.psum_scatter(row_ext, "node", scatter_dimension=0, tiled=True)
    back = lax.all_to_all(summed.reshape(col_count, per_rank, wide), "dev", 0, 0, tiled=True)
    back = jnp.sum(back.reshape(round_total, REPS, per_rank, wide), axis=1).reshape(row_slots, wide)
    back_tok = back[:, :model_width]
    back_hi = back_tok.astype(jnp.bfloat16)
    back_lo = (back_tok - back_hi.astype(jnp.float32)).astype(jnp.bfloat16)
    grad_tokens = jnp.einsum("qt,qd->td", pick_half, back_hi, preferred_element_type=jnp.float32)
    grad_tokens = grad_tokens + jnp.einsum(
        "qt,qd->td", pick_half, back_lo, preferred_element_type=jnp.float32
    )
    grad_tokens = grad_tokens.astype(jnp.bfloat16)
    back_q = back[:, model_width]
    rank_back = jnp.sum(jnp.where(chooser, back_q[:, None, None], 0.0), axis=0)
    grad_gates = jnp.sum(jnp.where(match, rank_back[:, None, :], 0.0), axis=-1)

    def home(cols):
        sent = cols.reshape(col_count, chunk, half)
        got = lax.all_to_all(sent, "dev", 0, 0, tiled=True).reshape(round_total, REPS, chunk, half)
        return jnp.concatenate([got[:, h] for h in range(REPS)], axis=-1)

    grad_w_gate = home(grad_gate_cols)
    grad_w_up = home(grad_up_cols)
    got_down = lax.all_to_all(
        grad_down_cols.reshape(col_count, chunk, half), "dev", 0, 0, tiled=True
    )
    got_down = got_down.reshape(round_total, REPS, chunk, half)
    grad_w_down = jnp.concatenate([jnp.swapaxes(got_down[:, h], 1, 2) for h in range(REPS)], axis=1)
    del node_count
    return (grad_tokens, grad_gates, grad_w_gate, grad_w_up, grad_w_down)


def solution(mesh):
    return jax.shard_map(
        local,
        mesh=mesh,
        in_specs=(
            P(("node", "dev"), None),
            P(("node", "dev"), None),
            P(("node", "dev"), None),
            P(("node", "dev"), None),
            P(),
            P(None, "dev", "node"),
            P(None, "dev", "node"),
            P(None, "node", "dev"),
        ),
        out_specs=(
            P(("node", "dev"), None),
            P(("node", "dev"), None),
            P(None, "dev", "node"),
            P(None, "dev", "node"),
            P(None, "node", "dev"),
        ),
        check_vma=False,
    )
```

profile of v0, /device:TPU:0, one launch (start us, length us, event | category | flops | bytes accessed | tf_op | source)
XLA Modules:
  0.0 319.0 jit_solution(12823636620467152112)
XLA Ops:
  16.0 33.8 %all_to_all.40 = bf16[16,4,14464]{2,1,0:T(4,128)(2,1)} all-to-all(bf16[16,4,14464]{2,1,0:T(4,128)(2,1)S(1)} %bitcast.58), channel_id=1, replica_groups=mesh['node'=8,'dev'=16] {'dev'}, dimensions={0} | all-to-all | bytes 3702784 | tf_op jit(solution)/shard_map/all_to_all | solution.py:77
  57.7 3.7 %all-to-all-start.3 = ((bf16[16,448,128]{2,1,0:T(8,128)(2,1)}), bf16[16,448,128]{2,1,0:T(8,128)(2,1)S(1)}, u32[]{:S(2)}, u32[]{:S(2)}) async-start(bf16[16,448,128]{2,1,0:T(8,128)(2,1)} %bitcast.63), calls=%async_computation.3 | async-start | bytes 3670016 | tf_op jit(solution)/shard_map/all_to_all | solution.py:54
  64.5 23.4 %all-to-all-done.3 = bf16[16,448,128]{2,1,0:T(8,128)(2,1)S(1)} async-done(((bf16[16,448,128]{2,1,0:T(8,128)(2,1)}), bf16[16,448,128]{2,1,0:T(8,128)(2,1)S(1)}, u32[]{:S(2)}, u32[]{:S(2)}) %all-to-all-start.3) | async-done | bytes 1835040 | tf_op jit(solution)/shard_map/all_to_all | solution.py:54
  88.0 4.4 %all-to-all-start.1 = ((bf16[16,448,128]{2,1,0:T(8,128)(2,1)}), bf16[16,448,128]{2,1,0:T(8,128)(2,1)}, u32[]{:S(2)}, u32[]{:S(2)}) async-start(bf16[16,448,128]{2,1,0:T(8,128)(2,1)} %bitcast.62), calls=%async_computation.1 | async-start | bytes 3670016 | tf_op jit(solution)/shard_map/all_to_all | solution.py:56
  95.4 23.1 %all-to-all-done.1 = bf16[16,448,128]{2,1,0:T(8,128)(2,1)} async-done(((bf16[16,448,128]{2,1,0:T(8,128)(2,1)}), bf16[16,448,128]{2,1,0:T(8,128)(2,1)}, u32[]{:S(2)}, u32[]{:S(2)}) %all-to-all-start.1) | async-done | bytes 1835040 | tf_op jit(solution)/shard_map/all_to_all | solution.py:56
  118.5 4.4 %all-to-all-start.2 = ((bf16[16,448,128]{2,1,0:T(8,128)(2,1)}), bf16[16,448,128]{2,1,0:T(8,128)(2,1)}, u32[]{:S(2)}, u32[]{:S(2)}) async-start(bf16[16,448,128]{2,1,0:T(8,128)(2,1)} %bitcast.61), calls=%async_computation.2 | async-start | bytes 3670016 | tf_op jit(solution)/shard_map/all_to_all | solution.py:55
  123.2 5.8 %fusion.40 = f32[512,128]{0,1:T(8,128)S(1)} fusion(bf16[512,7168]{1,0:T(8,128)(2,1)} %all-gather.5.cloned.1.call-done, bf16[7168,128]{1,0:T(8,128)(2,1)S(1)} %bitcast.56), kind=kOutput, calls=%fused_computation.101 | convolution fusion | flops 939524096 | bytes 9437184 | tf_op jit(solution)/shard_map/dot_general | solution.py:83
  129.0 15.7 %all-gather.3.cloned.1.call-done = bf16[512,7296]{1,0:T(8,128)(2,1)} async-done(((bf16[64,7296]{1,0:T(8,128)(2,1)}), bf16[512,7296]{1,0:T(8,128)(2,1)}) %all-gather.3.cloned.1.call-update) | async-done | bytes 7471120 | tf_op jit(solution)/shard_map/all_gather | solution.py:80
  145.7 6.1 %fusion.2 = f32[512,128]{0,1:T(8,128)S(1)} fusion(bf16[7168,128]{1,0:T(8,128)(2,1)} %bitcast.5, bf16[512,7296]{1,0:T(8,128)(2,1)} %all-gather.3.cloned.1.call-done), kind=kOutput, calls=%fused_computation.9 | convolution fusion | flops 939524096 | bytes 9437184 | tf_op jit(solution)/shard_map/dot_general | solution.py:85
  151.8 6.2 %broadcast_select_fusion.1 = (bf16[512,128]{0,1:T(8,128)(2,1)S(1)}, bf16[512,128]{0,1:T(8,128)(2,1)S(1)}, bf16[512,128]{0,1:T(8,128)(2,1)S(1)}, bf16[512,128]{0,...) fusion(pred[512]{0:T(512)(128)(4,1)S(1)} %fusion.28, ...), kind=kOutput, calls=%fused_computation.62 | convolution fusion | flops 940834816 | bytes 10750464 | tf_op jit(solution)/shard_map/dot_general | solution.py:84
  160.3 8.9 %select_add_fusion = f32[512,7296]{1,0:T(8,128)} fusion(f32[512,7296]{1,0:T(8,128)S(1)} %fusion.8, bf16[512,128]{0,1:T(8,128)(2,1)S(1)} %get-tuple-element.28, f32[512]{0:T(512)S(1)} %multiply_reduce_fusion, pred[7296]{0:T(1024)(128)(4,1)S(1)} %iota_compare_fusion.3, bf16[7168,128]{1,0:T(8,128)(2,1)} %bitcast.7), kind=kOutput, calls=%fused_computation | convolution fusion | flops 967507968 | bytes 31859840 | tf_op jit(solution)/shard_map/rh,dh->rd/dot_general | solution.py:117
  169.2 5.2 %convolution_reduce-precision_fusion = f32[7168,256]{1,0:T(8,128)S(1)} fusion(bf16[512,7296]{1,0:T(8,128)(2,1)} %all-gather.3.cloned.1.call-done, bf16[512,128]{0,1:T(8,128)(2,1)S(1)} %get-tuple-element.31, bf16[512,128]{0,1:T(8,128)(2,1)S(1)} %get-tuple-element.7), kind=kOutput, calls=%fused_computation.2 | convolution fusion | flops 1881407488 | bytes 14942208 | tf_op jit(solution)/shard_map/rd,rh->dh/dot_general | solution.py:106
  176.0 7.0 %all-to-all-start.7 = ((bf16[16,448,128]{2,1,0:T(8,128)(2,1)}), bf16[16,448,128]{2,1,0:T(8,128)(2,1)S(1)}, u32[]{:S(2)}, u32[]{:S(2)}) async-start(bf16[16,448,128]{2,1,0:T(8,128)(2,1)} %bitcast.66), calls=%async_computation.8 | async-start | bytes 3670016 | tf_op jit(solution)/shard_map/all_to_all | solution.py:144
  183.0 5.3 %convolution_reduce-precision_fusion.2 = f32[7168,256]{1,0:T(8,128)S(1)} fusion(bf16[512,7168]{1,0:T(8,128)(2,1)} %all-gather.5.cloned.1.call-done, bf16[512,128]{0,1:T(8,128)(2,1)S(1)} %get-tuple-element.32, bf16[512,128]{0,1:T(8,128)(2,1)S(1)} %get-tuple-element.25), kind=kOutput, calls=%fused_computation.4 | convolution fusion | flops 1881407488 | bytes 14942208 | tf_op jit(solution)/shard_map/rd,rh->dh/dot_general | solution.py:106
  189.9 22.3 %all-to-all-done.7 = bf16[16,448,128]{2,1,0:T(8,128)(2,1)S(1)} async-done(((bf16[16,448,128]{2,1,0:T(8,128)(2,1)}), bf16[16,448,128]{2,1,0:T(8,128)(2,1)S(1)}, u32[]{:S(2)}, u32[]{:S(2)}) %all-to-all-start.7) | async-done | bytes 1835040 | tf_op jit(solution)/shard_map/all_to_all | solution.py:144
  212.2 4.4 %all-to-all-start.5 = ((bf16[16,448,128]{2,1,0:T(8,128)(2,1)}), bf16[16,448,128]{2,1,0:T(8,128)(2,1)}, u32[]{:S(2)}, u32[]{:S(2)}) async-start(bf16[16,448,128]{2,1,0:T(8,128)(2,1)} %bitcast.64), calls=%async_computation.6 | async-start | bytes 3670016 | tf_op jit(solution)/shard_map/all_to_all | solution.py:139
  216.6 5.4 %convolution_reduce-precision_fusion.1 = f32[7168,256]{1,0:T(8,128)S(1)} fusion(bf16[512,7168]{1,0:T(8,128)(2,1)} %all-gather.5.cloned.1.call-done, bf16[512,128]{0,1:T(8,128)(2,1)S(1)} %get-tuple-element.33, bf16[512,128]{0,1:T(8,128)(2,1)S(1)} %get-tuple-element.27), kind=kOutput, calls=%fused_computation.3 | convolution fusion | flops 1881407488 | bytes 14942208 | tf_op jit(solution)/shard_map/rd,rh->dh/dot_general | solution.py:106
  223.6 20.3 %all-to-all-done.5 = bf16[16,448,128]{2,1,0:T(8,128)(2,1)} async-done(((bf16[16,448,128]{2,1,0:T(8,128)(2,1)}), bf16[16,448,128]{2,1,0:T(8,128)(2,1)}, u32[]{:S(2)}, u32[]{:S(2)}) %all-to-all-start.5) | async-done | bytes 1835040 | tf_op jit(solution)/shard_map/all_to_all | solution.py:139
  243.9 3.7 %all-to-all-start.6 = ((bf16[16,448,128]{2,1,0:T(8,128)(2,1)}), bf16[16,448,128]{2,1,0:T(8,128)(2,1)S(1)}, u32[]{:S(2)}, u32[]{:S(2)}) async-start(bf16[16,448,128]{2,1,0:T(8,128)(2,1)} %bitcast.65), calls=%async_computation.7 | async-start | bytes 3670016 | tf_op jit(solution)/shard_map/all_to_all | solution.py:139
  247.6 5.5 %reduce-scatter.2.cloned.1.call-done = f32[64,7296]{1,0:T(8,128)} async-done(((f32[512,7296]{1,0:T(8,128)}), f32[64,7296]{1,0:T(8,128)}) %reduce-scatter.2.cloned.1.call-update) | async-done | bytes 1867792 | tf_op jit(solution)/shard_map/reduce_scatter | solution.py:122
  255.9 18.5 %all-to-all-done.6 = bf16[16,448,128]{2,1,0:T(8,128)(2,1)S(1)} async-done(((bf16[16,448,128]{2,1,0:T(8,128)(2,1)}), bf16[16,448,128]{2,1,0:T(8,128)(2,1)S(1)}, u32[]{:S(2)}, u32[]{:S(2)}) %all-to-all-start.6) | async-done | bytes 1835040 | tf_op jit(solution)/shard_map/all_to_all | solution.py:139
  275.7 4.0 %all-to-all-start.4 = ((f32[16,4,7296]{2,1,0:T(4,128)}), f32[16,4,7296]{2,1,0:T(4,128)S(1)}, u32[]{:S(2)}, u32[]{:S(2)}) async-start(f32[16,4,7296]{2,1,0:T(4,128)} %reshape.146), calls=%async_computation.5 | async-start | bytes 3735552 | tf_op jit(solution)/shard_map/all_to_all | solution.py:123
  286.8 19.9 %all-to-all-done.4 = f32[16,4,7296]{2,1,0:T(4,128)S(1)} async-done(((f32[16,4,7296]{2,1,0:T(4,128)}), f32[16,4,7296]{2,1,0:T(4,128)S(1)}, u32[]{:S(2)}, u32[]{:S(2)}) %all-to-all-start.4) | async-done | bytes 1867808 | tf_op jit(solution)/shard_map/all_to_all | solution.py:123
  309.5 3.0 fusion
  (69 shorter events, 44.9 us)
Async XLA Ops:
  7.2 116.0 %all-gather.5.cloned.1.call-start = ((), (), s32[]{:S(2)}) async-start(), calls=%async_computation.10 | async-start | bytes 8257536 | tf_op jit(solution)/shard_map/all_gather | solution.py:79
  8.4 6.0 %copy-start.3 = (bf16[256,7168]{1,0:T(8,128)(2,1)S(1)}, bf16[256,7168]{1,0:T(8,128)(2,1)}, u32[]{:S(2)}) copy-start(bf16[256,7168]{1,0:T(8,128)(2,1)} %param.8) | copy-start | bytes 11010052
  53.7 91.0 %all-gather.3.cloned.1.call-start = ((), (), s32[]{:S(2)}) async-start(), calls=%async_computation.9 | async-start | bytes 8404992 | tf_op jit(solution)/shard_map/all_gather | solution.py:80
  57.7 30.3 %all-to-all-start.3 = ((bf16[16,448,128]{2,1,0:T(8,128)(2,1)}), bf16[16,448,128]{2,1,0:T(8,128)(2,1)S(1)}, u32[]{:S(2)}, u32[]{:S(2)}) async-start(bf16[16,448,128]{2,1,0:T(8,128)(2,1)} %bitcast.63), calls=%async_computation.3 | async-start | bytes 3670016 | tf_op jit(solution)/shard_map/all_to_all | solution.py:54
  88.0 30.5 %all-to-all-start.1 = ((bf16[16,448,128]{2,1,0:T(8,128)(2,1)}), bf16[16,448,128]{2,1,0:T(8,128)(2,1)}, u32[]{:S(2)}, u32[]{:S(2)}) async-start(bf16[16,448,128]{2,1,0:T(8,128)(2,1)} %bitcast.62), calls=%async_computation.1 | async-start | bytes 3670016 | tf_op jit(solution)/shard_map/all_to_all | solution.py:56
  118.5 33.3 %all-to-all-start.2 = ((bf16[16,448,128]{2,1,0:T(8,128)(2,1)}), bf16[16,448,128]{2,1,0:T(8,128)(2,1)}, u32[]{:S(2)}, u32[]{:S(2)}) async-start(bf16[16,448,128]{2,1,0:T(8,128)(2,1)} %bitcast.61), calls=%async_computation.2 | async-start | bytes 3670016 | tf_op jit(solution)/shard_map/all_to_all | solution.py:55
  122.9 130.2 %reduce-scatter.2.cloned.1.call-start = ((), (), s32[]{:S(2)}) async-start(), calls=%async_computation.11 | async-start | bytes 16809984 | tf_op jit(solution)/shard_map/reduce_scatter | solution.py:122
  176.0 36.2 %all-to-all-start.7 = ((bf16[16,448,128]{2,1,0:T(8,128)(2,1)}), bf16[16,448,128]{2,1,0:T(8,128)(2,1)S(1)}, u32[]{:S(2)}, u32[]{:S(2)}) async-start(bf16[16,448,128]{2,1,0:T(8,128)(2,1)} %bitcast.66), calls=%async_computation.8 | async-start | bytes 3670016 | tf_op jit(solution)/shard_map/all_to_all | solution.py:144
  212.2 9.8 %copy-start = (bf16[16,448,128]{2,1,0:T(8,128)(2,1)}, bf16[16,448,128]{2,1,0:T(8,128)(2,1)S(1)}, u32[]{:S(2)}) copy-start(bf16[16,448,128]{2,1,0:T(8,128)(2,1)S(1)} %all-to-all-done.7) | copy-start | bytes 5505028
  212.2 31.7 %all-to-all-start.5 = ((bf16[16,448,128]{2,1,0:T(8,128)(2,1)}), bf16[16,448,128]{2,1,0:T(8,128)(2,1)}, u32[]{:S(2)}, u32[]{:S(2)}) async-start(bf16[16,448,128]{2,1,0:T(8,128)(2,1)} %bitcast.64), calls=%async_computation.6 | async-start | bytes 3670016 | tf_op jit(solution)/shard_map/all_to_all | solution.py:139
  243.9 30.5 %all-to-all-start.6 = ((bf16[16,448,128]{2,1,0:T(8,128)(2,1)}), bf16[16,448,128]{2,1,0:T(8,128)(2,1)S(1)}, u32[]{:S(2)}, u32[]{:S(2)}) async-start(bf16[16,448,128]{2,1,0:T(8,128)(2,1)} %bitcast.65), calls=%async_computation.7 | async-start | bytes 3670016 | tf_op jit(solution)/shard_map/all_to_all | solution.py:139
  274.4 1.2 copy-start.1
  275.7 31.0 %all-to-all-start.4 = ((f32[16,4,7296]{2,1,0:T(4,128)}), f32[16,4,7296]{2,1,0:T(4,128)S(1)}, u32[]{:S(2)}, u32[]{:S(2)}) async-start(f32[16,4,7296]{2,1,0:T(4,128)} %reshape.146), calls=%async_computation.5 | async-start | bytes 3735552 | tf_op jit(solution)/shard_map/all_to_all | solution.py:123
  281.2 3.0 copy-start.2
  307.5 1.3 copy-start.4
Sparse Core Ops, SparseCore 0:
  53.8 42.6 all-gather.4
  98.7 45.8 all-gather.2
  169.3 83.7 reduce-scatter.1
where the time goes:
time: 320 us; the launch traced here: 319 us
  waiting for transfers between devices  149 us (47%)
  matrix products  52.8 us (16%)
  blocking collectives  33.8 us (11%)
  starting transfers between devices  32 us (10%)
  other arithmetic  19.1 us (6%)
  local copies, waits for them, and re-layouts  18.5 us (6%)
  between operations  14.1 us (4%)
    all_to_all x2, waiting for transfers between devices, home(): lax.all_to_all(sent, 'dev', 0, 0, tiled=True)  38.8 us
    all_to_all x1, blocking collectives, local(): lax.all_to_all(both.reshape(col_count, per_rank, both_width), 'dev', 0, 0...  33.8 us
    all_to_all x1, waiting for transfers between devices, local(): lax.all_to_all(send_wg, 'dev', 0, 0, tiled=True).reshape(model_width, half)  23.4 us
    all_to_all x1, waiting for transfers between devices, local(): lax.all_to_all(send_wd, 'dev', 0, 0, tiled=True).reshape(model_width, half)  23.1 us
    all_to_all x1, waiting for transfers between devices, local(): lax.all_to_all(grad_down_cols.reshape(col_count, chunk, half), 'dev', 0,...  22.3 us
    all_to_all x1, waiting for transfers between devices, local(): lax.all_to_all(summed.reshape(col_count, per_rank, wide), 'dev', 0, 0, ti...  19.9 us
    dot_general x3, matrix products, slot_pair_sum(): jnp.einsum('rd,rh->dh', rows, by_slot(d), preferred_element_type=jnp.floa...  15.9 us
    all_gather x1, waiting for transfers between devices, local(): dy_ext = lax.all_gather(both[:, model_width:], 'node', axis=0, tiled=True)  15.7 us
  transfers between devices with their start and end apart: 10, of which 8 were waited for; matrix products, arithmetic and copies ran while one was open for 17% of the time, Pallas kernels for 0%

commit v1 on v0

--- a/solution.py
+++ b/solution.py
@@ -7,6 +7,24 @@
 CAP = 2
 REPS = 2
 LANE = 128
+
+
+def gather_around(array, axis, dim):
+    ways, here, turn = (lax.axis_size(axis), lax.axis_index(axis), array.shape[dim])
+    dims = [n * ways if d == dim else n for d, n in enumerate(array.shape)]
+    full = lax.dynamic_update_slice_in_dim(
+        jnp.zeros(dims, array.dtype), array, here * turn, axis=dim
+    )
+    going_up = going_down = array
+    for far in range(1, ways // 2 + 1):
+        going_up = lax.ppermute(going_up, axis, [(d, (d + 1) % ways) for d in range(ways)])
+        full = lax.dynamic_update_slice_in_dim(full, going_up, (here - far) % ways * turn, axis=dim)
+        if 2 * far < ways:
+            going_down = lax.ppermute(going_down, axis, [(d, (d - 1) % ways) for d in range(ways)])
+            full = lax.dynamic_update_slice_in_dim(
+                full, going_down, (here + far) % ways * turn, axis=dim
+            )
+    return full
 
 
 def routing(expert_ids, slot_plan, slot_count, round_total):
@@ -77,7 +95,7 @@
     both = lax.all_to_all(both.reshape(col_count, per_rank, both_width), "dev", 0, 0, tiled=True)
     both = both.reshape(col_count * per_rank, both_width)
     x_rows = lax.all_gather(both[:, :model_width], "node", axis=0, tiled=True)
-    dy_ext = lax.all_gather(both[:, model_width:], "node", axis=0, tiled=True)
+    dy_ext = gather_around(both[:, model_width:], "node", 0)
     dy_rows = dy_ext[:, :model_width]
     gate_rows = dy_ext[:, model_width].astype(jnp.float32)[:, None]
     gate_pre = jnp.dot(x_rows, slot_gate, preferred_element_type=jnp.float32)

time: 320 us -> 511 us (1.60)
  the two profiles are of different devices: /device:TPU:0 before, /device:TPU:6 now
where the time goes in v1:
time: 511 us; the launch traced here: 505 us
  local copies, waits for them, and re-layouts  204 us (40%)
  waiting for transfers between devices  144 us (28%)
  matrix products  51 us (10%)
  starting transfers between devices  37.6 us (7%)
  blocking collectives  33.7 us (7%)
  other arithmetic  20.5 us (4%)
  between operations  14.5 us (3%)
    dynamic_update_slice x4, local copies, waits for them, and re-layouts, gather_around(): lax.dynamic_update_slice_in_dim(full, going_up, (here - far) % ways * tur...  81.7 us
    dynamic_update_slice x3, local copies, waits for them, and re-layouts, gather_around(): lax.dynamic_update_slice_in_dim(full, going_down, (here + far) % ways * t...  61.9 us
    all_to_all x2, waiting for transfers between devices, home(): lax.all_to_all(sent, 'dev', 0, 0, tiled=True)  49.8 us
    ppermute x4, waiting for transfers between devices, gather_around(): lax.ppermute(going_up, axis, [(d, (d + 1) % ways) for d in range(ways)])  35.1 us
    all_to_all x1, blocking collectives, local(): lax.all_to_all(both.reshape(col_count, per_rank, both_width), 'dev', 0, 0...  33.7 us
    all_to_all x1, waiting for transfers between devices, local(): lax.all_to_all(grad_down_cols.reshape(col_count, chunk, half), 'dev', 0,...  21.8 us
    all_to_all x1, waiting for transfers between devices, local(): lax.all_to_all(summed.reshape(col_count, per_rank, wide), 'dev', 0, 0, ti...  20.8 us
    dynamic_update_slice x1, local copies, waits for them, and re-layouts, gather_around(): lax.dynamic_update_slice_in_dim(jnp.zeros(dims, array.dtype), array, here...  18 us
  transfers between devices with their start and end apart: 16, of which 11 were waited for; matrix products, arithmetic and copies ran while one was open for 47% of the time, Pallas kernels for 0%

profile of v1, /device:TPU:6, one launch (start us, length us, event | category | flops | bytes accessed | tf_op | source)
XLA Modules:
  0.0 505.0 jit_solution(5759567112038671719)
XLA Ops:
  16.0 33.7 %all_to_all.40 = bf16[16,4,14464]{2,1,0:T(4,128)(2,1)} all-to-all(bf16[16,4,14464]{2,1,0:T(4,128)(2,1)S(1)} %bitcast.59), channel_id=1, replica_groups=mesh['node'=8,'dev'=16] {'dev'}, dimensions={0} | all-to-all | bytes 3702784 | tf_op jit(solution)/shard_map/all_to_all | solution.py:95
  65.4 16.5 %collective-permute-done = bf16[64,7296]{1,0:T(8,128)(2,1)} collective-permute-done((bf16[64,7296]{1,0:T(8,128)(2,1)S(1)}, bf16[64,7296]{1,0:T(8,128)(2,1)}, u32[]{:S(2)}, u32[]{:S(2)}) %collective-permute-start) | collective-permute-done | bytes 933920 | tf_op jit(solution)/shard_map/ppermute | solution.py:20
  84.8 10.0 %all-to-all-done.1 = bf16[16,448,128]{2,1,0:T(8,128)(2,1)} async-done(((bf16[16,448,128]{2,1,0:T(8,128)(2,1)}), bf16[16,448,128]{2,1,0:T(8,128)(2,1)}, u32[]{:S(2)}, u32[]{:S(2)}) %all-to-all-start.1) | async-done | bytes 1835040 | tf_op jit(solution)/shard_map/all_to_all | solution.py:74
  99.2 11.3 %collective-permute-done.2 = bf16[64,7296]{1,0:T(8,128)(2,1)} collective-permute-done((bf16[64,7296]{1,0:T(8,128)(2,1)}, bf16[64,7296]{1,0:T(8,128)(2,1)}, u32[]{:S(2)}, u32[]{:S(2)}) %collective-permute-start.2) | collective-permute-done | bytes 933920 | tf_op jit(solution)/shard_map/ppermute | solution.py:20
  116.4 7.4 %collective-permute-done.4 = bf16[64,7296]{1,0:T(8,128)(2,1)} collective-permute-done((bf16[64,7296]{1,0:T(8,128)(2,1)}, bf16[64,7296]{1,0:T(8,128)(2,1)}, u32[]{:S(2)}, u32[]{:S(2)}) %collective-permute-start.4) | collective-permute-done | bytes 933920 | tf_op jit(solution)/shard_map/ppermute | solution.py:20
  136.9 18.0 %dynamic_update_slice.24 = bf16[512,7296]{0,1:T(8,128)(2,1)} dynamic-update-slice(bf16[512,7296]{0,1:T(8,128)(2,1)} %broadcast_in_dim.177, bf16[64,7296]{0,1:T(8,128)(2,1)} %copy.37, s32[]{:T(128)S(6)} %select_n.127, s32[]{:T(128)} %constant.79.clone.1) | dynamic-update-slice | bytes 1867780 | tf_op jit(solution)/shard_map/dynamic_update_slice | solution.py:15
  157.5 21.9 %dynamic_update_slice.25 = bf16[512,7296]{0,1:T(8,128)(2,1)} dynamic-update-slice(bf16[512,7296]{0,1:T(8,128)(2,1)} %dynamic_update_slice.24, bf16[64,7296]{0,1:T(8,128)(2,1)} %copy.38, s32[]{:T(128)S(6)} %select_n.129, s32[]{:T(128)} %constant.79.clone.1) | dynamic-update-slice | bytes 1867780 | tf_op jit(solution)/shard_map/dynamic_update_slice | solution.py:21
  182.1 21.1 %dynamic_update_slice.26 = bf16[512,7296]{0,1:T(8,128)(2,1)} dynamic-update-slice(bf16[512,7296]{0,1:T(8,128)(2,1)} %dynamic_update_slice.25, bf16[64,7296]{0,1:T(8,128)(2,1)} %copy.39, s32[]{:T(128)S(6)} %select_n.131, s32[]{:T(128)} %constant.79.clone.1) | dynamic-update-slice | bytes 1867780 | tf_op jit(solution)/shard_map/dynamic_update_slice | solution.py:24
  205.9 18.9 %dynamic_update_slice.27 = bf16[512,7296]{0,1:T(8,128)(2,1)} dynamic-update-slice(bf16[512,7296]{0,1:T(8,128)(2,1)} %dynamic_update_slice.26, bf16[64,7296]{0,1:T(8,128)(2,1)} %copy.40, s32[]{:T(128)S(6)} %select_n.133, s32[]{:T(128)} %constant.79.clone.1) | dynamic-update-slice | bytes 1867780 | tf_op jit(solution)/shard_map/dynamic_update_slice | solution.py:21
  227.4 18.9 %dynamic_update_slice.28 = bf16[512,7296]{0,1:T(8,128)(2,1)} dynamic-update-slice(bf16[512,7296]{0,1:T(8,128)(2,1)} %dynamic_update_slice.27, bf16[64,7296]{0,1:T(8,128)(2,1)} %copy.41, s32[]{:T(128)S(6)} %select_n.135, s32[]{:T(128)} %constant.79.clone.1) | dynamic-update-slice | bytes 1867780 | tf_op jit(solution)/shard_map/dynamic_update_slice | solution.py:24
  249.0 21.9 %dynamic_update_slice.29 = bf16[512,7296]{0,1:T(8,128)(2,1)} dynamic-update-slice(bf16[512,7296]{0,1:T(8,128)(2,1)} %dynamic_update_slice.28, bf16[64,7296]{0,1:T(8,128)(2,1)} %copy.42, s32[]{:T(128)S(6)} %select_n.137, s32[]{:T(128)} %constant.79.clone.1) | dynamic-update-slice | bytes 1867780 | tf_op jit(solution)/shard_map/dynamic_update_slice | solution.py:21
  273.6 21.9 %dynamic_update_slice.30 = bf16[512,7296]{0,1:T(8,128)(2,1)} dynamic-update-slice(bf16[512,7296]{0,1:T(8,128)(2,1)} %dynamic_update_slice.29, bf16[64,7296]{0,1:T(8,128)(2,1)} %copy.43, s32[]{:T(128)S(6)} %select_n.139, s32[]{:T(128)} %constant.79.clone.1) | dynamic-update-slice | bytes 1867780 | tf_op jit(solution)/shard_map/dynamic_update_slice | solution.py:24
  298.2 18.9 %dynamic_update_slice.31 = bf16[512,7296]{0,1:T(8,128)(2,1)} dynamic-update-slice(bf16[512,7296]{0,1:T(8,128)(2,1)} %dynamic_update_slice.30, bf16[64,7296]{0,1:T(8,128)(2,1)} %copy.44, s32[]{:T(128)S(6)} %select_n.141, s32[]{:T(128)} %constant.79.clone.1) | dynamic-update-slice | bytes 1867780 | tf_op jit(solution)/shard_map/dynamic_update_slice | solution.py:21
  322.6 5.6 %fusion.40 = f32[512,128]{0,1:T(8,128)S(1)} fusion(bf16[512,7168]{1,0:T(8,128)(2,1)} %all-gather.2.cloned.1.call-done, bf16[7168,128]{1,0:T(8,128)(2,1)S(1)} %bitcast.57), kind=kOutput, calls=%fused_computation.101 | convolution fusion | flops 939524096 | bytes 9437184 | tf_op jit(solution)/shard_map/dot_general | solution.py:101
  328.2 6.2 %broadcast_select_fusion.1 = (bf16[512,128]{0,1:T(8,128)(2,1)S(1)}, bf16[512,128]{0,1:T(8,128)(2,1)S(1)}, bf16[512,128]{0,1:T(8,128)(2,1)S(1)}, bf16[512,128]{0,...) fusion(pred[512]{0:T(512)(128)(4,1)S(1)} %fusion.28, ...), kind=kOutput, calls=%fused_computation.61 | convolution fusion | flops 940834816 | bytes 10750464 | tf_op jit(solution)/shard_map/dot_general | solution.py:102
  336.7 8.7 %select_add_fusion = f32[512,7296]{1,0:T(8,128)} fusion(f32[512,7296]{1,0:T(8,128)S(1)} %fusion.8, bf16[512,128]{0,1:T(8,128)(2,1)S(1)} %get-tuple-element.28, f32[512]{0:T(512)S(1)} %multiply_reduce_fusion, pred[7296]{0:T(1024)(128)(4,1)S(1)} %iota_compare_fusion.3, bf16[7168,128]{1,0:T(8,128)(2,1)} %bitcast.8), kind=kOutput, calls=%fused_computation | convolution fusion | flops 967507968 | bytes 31859840 | tf_op jit(solution)/shard_map/rh,dh->rd/dot_general | solution.py:135
  345.4 5.2 %convolution_reduce-precision_fusion = f32[7168,256]{1,0:T(8,128)S(1)} fusion(bf16[512,7296]{0,1:T(8,128)(2,1)} %dynamic_update_slice.31, bf16[512,128]{0,1:T(8,128)(2,1)S(1)} %get-tuple-element.31, bf16[512,128]{0,1:T(8,128)(2,1)S(1)} %get-tuple-element.7), kind=kOutput, calls=%fused_computation.2 | convolution fusion | flops 1881407488 | bytes 14942208 | tf_op jit(solution)/shard_map/rd,rh->dh/dot_general | solution.py:124
  352.2 7.1 %all-to-all-start.7 = ((bf16[16,448,128]{2,1,0:T(8,128)(2,1)}), bf16[16,448,128]{2,1,0:T(8,128)(2,1)S(1)}, u32[]{:S(2)}, u32[]{:S(2)}) async-start(bf16[16,448,128]{2,1,0:T(8,128)(2,1)} %bitcast.65), calls=%async_computation.8 | async-start | bytes 3670016 | tf_op jit(solution)/shard_map/all_to_all | solution.py:162
  359.3 5.2 %convolution_reduce-precision_fusion.1 = f32[7168,256]{1,0:T(8,128)S(1)} fusion(bf16[512,7168]{1,0:T(8,128)(2,1)} %all-gather.2.cloned.1.call-done, bf16[512,128]{0,1:T(8,128)(2,1)S(1)} %get-tuple-element.33, bf16[512,128]{0,1:T(8,128)(2,1)S(1)} %get-tuple-element.27), kind=kOutput, calls=%fused_computation.3 | convolution fusion | flops 1881407488 | bytes 14942208 | tf_op jit(solution)/shard_map/rd,rh->dh/dot_general | solution.py:124
  366.2 21.8 %all-to-all-done.7 = bf16[16,448,128]{2,1,0:T(8,128)(2,1)S(1)} async-done(((bf16[16,448,128]{2,1,0:T(8,128)(2,1)}), bf16[16,448,128]{2,1,0:T(8,128)(2,1)S(1)}, u32[]{:S(2)}, u32[]{:S(2)}) %all-to-all-start.7) | async-done | bytes 1835040 | tf_op jit(solution)/shard_map/all_to_all | solution.py:162
  392.4 5.4 %convolution_reduce-precision_fusion.2 = f32[7168,256]{1,0:T(8,128)S(1)} fusion(bf16[512,7168]{1,0:T(8,128)(2,1)} %all-gather.2.cloned.1.call-done, bf16[512,128]{0,1:T(8,128)(2,1)S(1)} %get-tuple-element.32, bf16[512,128]{0,1:T(8,128)(2,1)S(1)} %get-tuple-element.25), kind=kOutput, calls=%fused_computation.4 | convolution fusion | flops 1881407488 | bytes 14942208 | tf_op jit(solution)/shard_map/rd,rh->dh/dot_general | solution.py:124
  399.3 24.7 %all-to-all-done.6 = bf16[16,448,128]{2,1,0:T(8,128)(2,1)} async-done(((bf16[16,448,128]{2,1,0:T(8,128)(2,1)}), bf16[16,448,128]{2,1,0:T(8,128)(2,1)}, u32[]{:S(2)}, u32[]{:S(2)}) %all-to-all-start.6) | async-done | bytes 1835040 | tf_op jit(solution)/shard_map/all_to_all | solution.py:157
  433.4 25.1 %all-to-all-done.5 = bf16[16,448,128]{2,1,0:T(8,128)(2,1)} async-done(((bf16[16,448,128]{2,1,0:T(8,128)(2,1)}), bf16[16,448,128]{2,1,0:T(8,128)(2,1)}, u32[]{:S(2)}, u32[]{:S(2)}) %all-to-all-start.5) | async-done | bytes 1835040 | tf_op jit(solution)/shard_map/all_to_all | solution.py:157
  470.0 20.8 %all-to-all-done.4 = f32[16,4,7296]{2,1,0:T(4,128)} async-done(((f32[16,4,7296]{2,1,0:T(4,128)}), f32[16,4,7296]{2,1,0:T(4,128)}, u32[]{:S(2)}, u32[]{:S(2)}) %all-to-all-start.4) | async-done | bytes 1867808 | tf_op jit(solution)/shard_map/all_to_all | solution.py:141
  (93 shorter events, 114.5 us)
Async XLA Ops:
  7.2 315.4 %all-gather.2.cloned.1.call-start = ((), (), s32[]{:S(2)}) async-start(), calls=%async_computation.9 | async-start | bytes 8257536 | tf_op jit(solution)/shard_map/all_gather | solution.py:97
  8.4 6.0 %copy-start.1 = (bf16[256,7168]{1,0:T(8,128)(2,1)S(1)}, bf16[256,7168]{1,0:T(8,128)(2,1)}, u32[]{:S(2)}) copy-start(bf16[256,7168]{1,0:T(8,128)(2,1)} %param.8) | copy-start | bytes 11010052
  55.7 2.1 copy-start
  57.9 24.0 %collective-permute-start = (bf16[64,7296]{1,0:T(8,128)(2,1)S(1)}, bf16[64,7296]{1,0:T(8,128)(2,1)}, u32[]{:S(2)}, u32[]{:S(2)}) collective-permute-start(bf16[64,7296]{1,0:T(8,128)(2,1)S(1)} %slice.109), channel_id=1, source_target_pairs={{0,16},{16,32},{32,48},{48,64},{64,80},{80,96},{96,112},{112,0},{1... | collective-permute-start | bytes 2801672 | tf_op jit(solution)/shard_map/ppermute | solution.py:20
  59.2 35.6 %all-to-all-start.1 = ((bf16[16,448,128]{2,1,0:T(8,128)(2,1)}), bf16[16,448,128]{2,1,0:T(8,128)(2,1)}, u32[]{:S(2)}, u32[]{:S(2)}) async-start(bf16[16,448,128]{2,1,0:T(8,128)(2,1)} %bitcast.5), calls=%async_computation.1 | async-start | bytes 3670016 | tf_op jit(solution)/shard_map/all_to_all | solution.py:74
  63.7 34.9 %collective-permute-start.1 = (bf16[64,7296]{1,0:T(8,128)(2,1)S(1)}, bf16[64,7296]{1,0:T(8,128)(2,1)}, u32[]{:S(2)}, u32[]{:S(2)}) collective-permute-start(bf16[64,7296]{1,0:T(8,128)(2,1)S(1)} %slice.109), channel_id=1, source_target_pairs={{0,112},{16,0},{32,16},{48,32},{64,48},{80,64},{96,80},{112,96},{1... | collective-permute-start | bytes 2801672 | tf_op jit(solution)/shard_map/ppermute | solution.py:23
  81.9 28.6 %collective-permute-start.2 = (bf16[64,7296]{1,0:T(8,128)(2,1)}, bf16[64,7296]{1,0:T(8,128)(2,1)}, u32[]{:S(2)}, u32[]{:S(2)}) collective-permute-start(bf16[64,7296]{1,0:T(8,128)(2,1)} %collective-permute-done), channel_id=1, source_target_pairs={{0,16},{16,32},{32,48},{48,64},{64,80},{80,96},{96,112},{112,0},{1... | collective-permute-start | bytes 2801672 | tf_op jit(solution)/shard_map/ppermute | solution.py:20
  94.8 32.2 %all-to-all-start.3 = ((bf16[16,448,128]{2,1,0:T(8,128)(2,1)}), bf16[16,448,128]{2,1,0:T(8,128)(2,1)S(1)}, u32[]{:S(2)}, u32[]{:S(2)}) async-start(bf16[16,448,128]{2,1,0:T(8,128)(2,1)} %bitcast.62), calls=%async_computation.3 | async-start | bytes 3670016 | tf_op jit(solution)/shard_map/all_to_all | solution.py:72
  98.5 15.7 %collective-permute-start.3 = (bf16[64,7296]{1,0:T(8,128)(2,1)}, bf16[64,7296]{1,0:T(8,128)(2,1)}, u32[]{:S(2)}, u32[]{:S(2)}) collective-permute-start(bf16[64,7296]{1,0:T(8,128)(2,1)} %collective-permute-done.1), channel_id=1, source_target_pairs={{0,112},{16,0},{32,16},{48,32},{64,48},{80,64},{96,80},{112,96},{1... | collective-permute-start | bytes 2801672 | tf_op jit(solution)/shard_map/ppermute | solution.py:23
  110.5 13.3 %collective-permute-start.4 = (bf16[64,7296]{1,0:T(8,128)(2,1)}, bf16[64,7296]{1,0:T(8,128)(2,1)}, u32[]{:S(2)}, u32[]{:S(2)}) collective-permute-start(bf16[64,7296]{1,0:T(8,128)(2,1)} %collective-permute-done.2), channel_id=1, source_target_pairs={{0,16},{16,32},{32,48},{48,64},{64,80},{80,96},{96,112},{112,0},{1... | collective-permute-start | bytes 2801672 | tf_op jit(solution)/shard_map/ppermute | solution.py:20
  114.2 156.7 %collective-permute-start.5 = (bf16[64,7296]{1,0:T(8,128)(2,1)}, bf16[64,7296]{1,0:T(8,128)(2,1)}, u32[]{:S(2)}, u32[]{:S(2)}) collective-permute-start(bf16[64,7296]{1,0:T(8,128)(2,1)} %collective-permute-done.3), channel_id=1, source_target_pairs={{0,112},{16,0},{32,16},{48,32},{64,48},{80,64},{96,80},{112,96},{1... | collective-permute-start | bytes 2801672 | tf_op jit(solution)/shard_map/ppermute | solution.py:23
  123.8 171.7 %collective-permute-start.6 = (bf16[64,7296]{1,0:T(8,128)(2,1)}, bf16[64,7296]{1,0:T(8,128)(2,1)}, u32[]{:S(2)}, u32[]{:S(2)}) collective-permute-start(bf16[64,7296]{1,0:T(8,128)(2,1)} %collective-permute-done.4), channel_id=1, source_target_pairs={{0,16},{16,32},{32,48},{48,64},{64,80},{80,96},{96,112},{112,0},{1... | collective-permute-start | bytes 2801672 | tf_op jit(solution)/shard_map/ppermute | solution.py:20
  127.0 201.2 %all-to-all-start.2 = ((bf16[16,448,128]{2,1,0:T(8,128)(2,1)}), bf16[16,448,128]{2,1,0:T(8,128)(2,1)}, u32[]{:S(2)}, u32[]{:S(2)}) async-start(bf16[16,448,128]{2,1,0:T(8,128)(2,1)} %bitcast.60), calls=%async_computation.2 | async-start | bytes 3670016 | tf_op jit(solution)/shard_map/all_to_all | solution.py:73
  131.4 299.1 %reduce-scatter.2.cloned.1.call-start = ((), (), s32[]{:S(2)}) async-start(), calls=%async_computation.10 | async-start | bytes 16809984 | tf_op jit(solution)/shard_map/reduce_scatter | solution.py:140
  352.2 35.7 %all-to-all-start.7 = ((bf16[16,448,128]{2,1,0:T(8,128)(2,1)}), bf16[16,448,128]{2,1,0:T(8,128)(2,1)S(1)}, u32[]{:S(2)}, u32[]{:S(2)}) async-start(bf16[16,448,128]{2,1,0:T(8,128)(2,1)} %bitcast.65), calls=%async_computation.8 | async-start | bytes 3670016 | tf_op jit(solution)/shard_map/all_to_all | solution.py:162
  387.9 36.1 %all-to-all-start.6 = ((bf16[16,448,128]{2,1,0:T(8,128)(2,1)}), bf16[16,448,128]{2,1,0:T(8,128)(2,1)}, u32[]{:S(2)}, u32[]{:S(2)}) async-start(bf16[16,448,128]{2,1,0:T(8,128)(2,1)} %bitcast.63), calls=%async_computation.7 | async-start | bytes 3670016 | tf_op jit(solution)/shard_map/all_to_all | solution.py:157
  424.0 34.4 %all-to-all-start.5 = ((bf16[16,448,128]{2,1,0:T(8,128)(2,1)}), bf16[16,448,128]{2,1,0:T(8,128)(2,1)}, u32[]{:S(2)}, u32[]{:S(2)}) async-start(bf16[16,448,128]{2,1,0:T(8,128)(2,1)} %bitcast.64), calls=%async_computation.6 | async-start | bytes 3670016 | tf_op jit(solution)/shard_map/all_to_all | solution.py:157
  458.4 32.3 %all-to-all-start.4 = ((f32[16,4,7296]{2,1,0:T(4,128)}), f32[16,4,7296]{2,1,0:T(4,128)}, u32[]{:S(2)}, u32[]{:S(2)}) async-start(f32[16,4,7296]{2,1,0:T(4,128)} %reshape.146), calls=%async_computation.5 | async-start | bytes 3735552 | tf_op jit(solution)/shard_map/all_to_all | solution.py:141
  494.4 3.1 copy-start.2
Sparse Core Ops, SparseCore 0:
  55.9 53.8 all-gather.1
  345.5 84.9 reduce-scatter.1
